TPU v7x, 128 devices: a whole 4x4x4 slice. The times are simulated.
128 devices in a mesh: ctx: 16 (over z, y_hi, core), tp: 8 (over x, y_lo).
Axes of the slice: x: 4, y: 4 (y_hi: 2, y_lo: 2; y = y_hi * 2 + y_lo), z: 4, core: 2. Of those that a mesh axis runs over, the one named last changes fastest.
Arguments:
- queries: bfloat16 [16384, 2048], P('ctx', 'tp'), may hold values from -8 to 8
- keys: bfloat16 [16384, 2048], P('ctx', 'tp'), may hold values from -8 to 8
- values: bfloat16 [16384, 2048], P('ctx', 'tp'), may hold values from -6 to 6
- out_weight: bfloat16 [2048, 4096], P('tp'), may hold values from -0.125 to 0.125
- cotangent: bfloat16 [16384, 4096], P('ctx', 'tp'), may hold values from -6 to 6
- block_keep: int32 [16, 16], replicated, may hold values 0 or 1
Outputs:
- mixed: bfloat16 [16384, 4096], P('ctx', 'tp')
- d_queries: float32 [16384, 2048], P('ctx', 'tp')
- d_keys: float32 [16384, 2048], P('ctx', 'tp')
- d_values: float32 [16384, 2048], P('ctx', 'tp')
- d_weight: float32 [2048, 4096], P('tp', 'ctx')
All inputs are finite; a program needn't handle non-finite values.
Results may differ from a plain program's by a relative error of at most 0.014.
Values may be sent and summed in bfloat16 or wider, within the bound.
No kernel may reach another device: no remote copies, remote signals or barrier semaphores. Data moves between devices by JAX's collectives and lax.ppermute only.
A program may use at most 192 MiB of HBM per device.

v0:
```python
import functools
import math

import jax
import jax.numpy as jnp
from jax import lax
from jax.experimental import pallas as pl
from jax.experimental.pallas import tpu as pltpu
from jax.sharding import PartitionSpec as P

DH = 128
NEG = -1e30
KEY_TILE = 512


def passed_along(value, axis, steps):
    count = lax.axis_size(axis)
    initial, last = (max(0, -steps), min(count, count - steps))
    return lax.ppermute(value, axis, [(source, source + steps) for source in range(initial, last)])


def gathered(piece, axis):
    count = lax.axis_size(axis)
    spread = jnp.broadcast_to(piece[None], (count,) + piece.shape)
    parts = lax.all_to_all(spread, axis, 0, 0, tiled=True)
    return jnp.moveaxis(parts, 0, 1).reshape(piece.shape[0], count * piece.shape[1])


def summed_scatter(part, axis):
    count = lax.axis_size(axis)
    rows, cols = part.shape
    pieces = part.reshape(rows, count, cols // count)
    parts = lax.all_to_all(pieces, axis, 1, 1, tiled=True)
    return jnp.sum(parts.astype(jnp.float32), axis=1)


def masked_scores(flag_ref, q, k, step, tiles, scale):
    block = step // tiles
    tile = step % tiles
    raw = lax.dot_general(q, k, (((1,), (1,)), ((), ())), preferred_element_type=jnp.float32) * scale
    rows = lax.broadcasted_iota(jnp.int32, raw.shape, 0)
    cols = lax.broadcasted_iota(jnp.int32, raw.shape, 1) + tile * raw.shape[1]
    reach = 1 << 20
    offset = jnp.where(block == 0, 0, jnp.where(flag_ref[block] == 1, reach, -reach))
    return jnp.where(rows + offset >= cols, raw, NEG)


def forward_kernel(flag_ref, q_ref, k_ref, v_ref, att_ref, m_ref, l_ref, m_sc, l_sc, acc_sc, *, tiles, steps, scale):
    phase = pl.program_id(1)
    step = pl.program_id(2)
    scores = masked_scores(flag_ref, q_ref[...], k_ref[...], step, tiles, scale)

    @pl.when((phase == 0) & (step == 0))
    def _():
        m_sc[...] = jnp.full(m_sc.shape, NEG, jnp.float32)
        l_sc[...] = jnp.zeros(l_sc.shape, jnp.float32)

    @pl.when(phase == 0)
    def _():
        old = m_sc[...]
        new = jnp.maximum(old, jnp.max(scores, axis=1, keepdims=True))
        l_sc[...] = l_sc[...] * jnp.exp(old - new) + jnp.sum(jnp.exp(scores - new), axis=1, keepdims=True)
        m_sc[...] = new

    @pl.when((phase == 1) & (step == 0))
    def _():
        acc_sc[...] = jnp.zeros(acc_sc.shape, jnp.float32)

    @pl.when(phase == 1)
    def _():
        probs = jnp.exp(scores - m_sc[...]) * (1.0 / l_sc[...])
        acc_sc[...] += jnp.dot(probs.astype(jnp.bfloat16), v_ref[...], preferred_element_type=jnp.float32)

    @pl.when((phase == 1) & (step == steps - 1))
    def _():
        att_ref[...] = acc_sc[...]
        m_ref[...] = jnp.broadcast_to(m_sc[...], m_ref.shape)
        l_ref[...] = jnp.broadcast_to(l_sc[...], l_ref.shape)


def backward_kernel(
    flag_ref, q_ref, k_ref, v_ref, g_ref, att_ref, m_ref, l_ref, dq_ref, dk_ref, dv_ref, dq_sc, *, tiles, steps, scale
):
    step = pl.program_id(1)
    q = q_ref[...]
    k = k_ref[...]
    g = g_ref[...]
    scores = masked_scores(flag_ref, q, k, step, tiles, scale)
    probs = jnp.exp(scores - m_ref[:, :1]) * (1.0 / l_ref[:, :1])
    weights = probs.astype(jnp.bfloat16)
    dots = lax.dot_general(g, v_ref[...], (((1,), (1,)), ((), ())), preferred_element_type=jnp.float32)
    delta = jnp.sum(g.astype(jnp.float32) * att_ref[...], axis=1, keepdims=True)
    slopes = (probs * (dots - delta) * scale).astype(jnp.bfloat16)

    @pl.when(step == 0)
    def _():
        dq_sc[...] = jnp.zeros(dq_sc.shape, jnp.float32)

    dq_sc[...] += jnp.dot(slopes, k, preferred_element_type=jnp.float32)
    dk_ref[...] = lax.dot_general(slopes, q, (((0,), (0,)), ((), ())), preferred_element_type=jnp.float32)
    dv_ref[...] = lax.dot_general(weights, g, (((0,), (0,)), ((), ())), preferred_element_type=jnp.float32)

    @pl.when(step == steps - 1)
    def _():
        dq_ref[...] = dq_sc[...]


def attention_forward(flags, queries, keys_all, values_all, scale):
    nblocks, block_len, cols = keys_all.shape
    heads = cols // DH
    tiles = block_len // KEY_TILE
    steps = nblocks * tiles
    q_spec = pl.BlockSpec((block_len, DH), lambda h, ph, s, f: (0, h))
    k_spec = pl.BlockSpec((None, KEY_TILE, DH), lambda h, ph, s, f: (s // tiles, s % tiles, h))
    v_spec = pl.BlockSpec((None, KEY_TILE, DH), lambda h, ph, s, f: ((s // tiles) * ph, (s % tiles) * ph, h))
    stat_spec = pl.BlockSpec((None, block_len, DH), lambda h, ph, s, f: (h, 0, 0))
    kernel = functools.partial(forward_kernel, tiles=tiles, steps=steps, scale=scale)
    return pl.pallas_call(
        kernel,
        grid_spec=pltpu.PrefetchScalarGridSpec(
            num_scalar_prefetch=1,
            grid=(heads, 2, steps),
            in_specs=[q_spec, k_spec, v_spec],
            out_specs=[q_spec, stat_spec, stat_spec],
            scratch_shapes=[
                pltpu.VMEM((block_len, 1), jnp.float32),
                pltpu.VMEM((block_len, 1), jnp.float32),
                pltpu.VMEM((block_len, DH), jnp.float32),
            ],
        ),
        out_shape=[
            jax.ShapeDtypeStruct((block_len, cols), jnp.float32),
            jax.ShapeDtypeStruct((heads, block_len, DH), jnp.float32),
            jax.ShapeDtypeStruct((heads, block_len, DH), jnp.float32),
        ],
        compiler_params=pltpu.CompilerParams(dimension_semantics=("arbitrary", "arbitrary", "arbitrary")),
    )(flags, queries, keys_all, values_all)


def attention_backward(flags, queries, keys_all, values_all, grads, attended32, row_max, row_total, scale):
    nblocks, block_len, cols = keys_all.shape
    heads = cols // DH
    tiles = block_len // KEY_TILE
    steps = nblocks * tiles
    q_spec = pl.BlockSpec((block_len, DH), lambda h, s, f: (0, h))
    k_spec = pl.BlockSpec((None, KEY_TILE, DH), lambda h, s, f: (s // tiles, s % tiles, h))
    stat_spec = pl.BlockSpec((None, block_len, DH), lambda h, s, f: (h, 0, 0))
    kernel = functools.partial(backward_kernel, tiles=tiles, steps=steps, scale=scale)
    return pl.pallas_call(
        kernel,
        grid_spec=pltpu.PrefetchScalarGridSpec(
            num_scalar_prefetch=1,
            grid=(heads, steps),
            in_specs=[q_spec, k_spec, k_spec, q_spec, q_spec, stat_spec, stat_spec],
            out_specs=[q_spec, k_spec, k_spec],
            scratch_shapes=[pltpu.VMEM((block_len, DH), jnp.float32)],
        ),
        out_shape=[
            jax.ShapeDtypeStruct((block_len, cols), jnp.float32),
            jax.ShapeDtypeStruct((nblocks, block_len, cols), jnp.float32),
            jax.ShapeDtypeStruct((nblocks, block_len, cols), jnp.float32),
        ],
        compiler_params=pltpu.CompilerParams(dimension_semantics=("arbitrary", "arbitrary")),
    )(flags, queries, keys_all, values_all, grads, attended32, row_max, row_total)


def local(queries, keys, values, out_weight, cotangent, block_keep):
    block_len = queries.shape[0]
    local_cols = queries.shape[1]
    score_scale = 1.0 / math.sqrt(DH)
    axis_len = lax.axis_size("ctx")
    levels = axis_len.bit_length() - 1
    block_index = lax.axis_index("ctx")
    stacked = jnp.stack([keys, values])
    remote = [passed_along(stacked, "ctx", 1 << level) for level in range(levels)]
    blocks = [stacked] + remote
    keys_all = jnp.stack([b[0] for b in blocks])
    values_all = jnp.stack([b[1] for b in blocks])
    row_pick = lax.broadcasted_iota(jnp.int32, block_keep.shape, 0) == block_index
    keep_row = jnp.sum(jnp.where(row_pick, block_keep, 0), axis=0)
    column_ids = lax.broadcasted_iota(jnp.int32, keep_row.shape, 0)
    flags = [jnp.array(True)]
    for level in range(levels):
        target = block_index - (1 << level)
        linked = jnp.sum(jnp.where(column_ids == target, keep_row, 0))
        flags.append((target >= 0) & (linked == 1))
    flags = jnp.stack(flags).astype(jnp.int32)

    attended32, row_max, row_total = attention_forward(flags, queries, keys_all, values_all, score_scale)
    attended = attended32.astype(jnp.bfloat16)
    weight_cols = lax.all_to_all(out_weight, "tp", split_axis=1, concat_axis=0, tiled=True)
    mixed_sum = jnp.dot(gathered(attended, "tp"), weight_cols, preferred_element_type=jnp.float32)
    mixed = mixed_sum.astype(jnp.bfloat16)
    piece = gathered(cotangent, "tp")
    grad_att = lax.dot_general(
        piece, out_weight, (((1,), (1,)), ((), ())), preferred_element_type=jnp.float32
    )
    weight_part = lax.dot_general(
        attended, piece, (((0,), (0,)), ((), ())), preferred_element_type=jnp.float32
    )
    d_weight = summed_scatter(weight_part.astype(jnp.bfloat16), "ctx")
    grad_heads = grad_att.astype(jnp.bfloat16)
    grad_query, key_grads, value_grads = attention_backward(
        flags, queries, keys_all, values_all, grad_heads, attended32, row_max, row_total, score_scale
    )
    own_key = key_grads[0]
    own_value = value_grads[0]
    for level in range(levels):
        back = jnp.stack([key_grads[level + 1], value_grads[level + 1]]).astype(jnp.bfloat16)
        arrived = passed_along(back, "ctx", -(1 << level)).astype(jnp.float32)
        own_key = own_key + arrived[0]
        own_value = own_value + arrived[1]
    return (mixed, grad_query, own_key, own_value, d_weight)


def solution(mesh):
    in_specs = (P("ctx", "tp"), P("ctx", "tp"), P("ctx", "tp"), P("tp", None), P("ctx", "tp"), P())
    out_specs = (P("ctx", "tp"), P("ctx", "tp"), P("ctx", "tp"), P("ctx", "tp"), P("tp", "ctx"))
    return jax.shard_map(local, mesh=mesh, in_specs=in_specs, out_specs=out_specs, check_vma=False)
```

profile of v0, /device:TPU:56, one launch (start us, length us, event | category | flops | bytes accessed | tf_op | source)
XLA Modules:
  0.0 427.8 jit_solution(6301493439258862597)
XLA Ops:
  0.6 3.3 copy.14
  3.9 2.4 copy.15
  6.3 5.8 %all-to-all-start.1 = ((bf16[256,8,512]{2,0,1:T(8,128)(2,1)}), bf16[256,8,512]{2,0,1:T(8,128)(2,1)S(1)}, u32[]{:S(2)}, u32[]{:S(2)}) async-start(bf16[256,8,512]{2,0,1:T(8,128)(2,1)} %copy.15), calls=%async_computation.1 | async-start | bytes 4194304 | tf_op jit(solution)/shard_map/all_to_all | solution.py:191
  12.1 1.5 copy.16
  13.6 27.8 %all-to-all-done.1 = bf16[256,8,512]{2,0,1:T(8,128)(2,1)S(1)} async-done(((bf16[256,8,512]{2,0,1:T(8,128)(2,1)}), bf16[256,8,512]{2,0,1:T(8,128)(2,1)S(1)}, u32[]{:S(2)}, u32[]{:S(2)}) %all-to-all-start.1) | async-done | bytes 2097184 | tf_op jit(solution)/shard_map/all_to_all | solution.py:191
  41.4 4.3 %broadcast_in_dim.26 = bf16[8,1024,512]{1,2,0:T(8,128)(2,1)} broadcast(bf16[1024,512]{0,1:T(8,128)(2,1)S(1)} %copy.16), dimensions={1,2} | broadcast | bytes 9437184 | tf_op jit(solution)/shard_map/broadcast_in_dim | solution.py:24
  45.8 6.9 %all-to-all-start.2 = ((bf16[8,1024,512]{1,2,0:T(8,128)(2,1)}), bf16[8,1024,512]{1,2,0:T(8,128)(2,1)}, u32[]{:S(2)}, u32[]{:S(2)}) async-start(bf16[8,1024,512]{1,2,0:T(8,128)(2,1)} %broadcast_in_dim.26), calls=%async_computation.2 | async-start | bytes 16777216 | tf_op jit(solution)/shard_map/all_to_all | solution.py:25
  53.7 1.9 collective-permute-start
  55.6 4.5 %collective-permute-start.1 = (bf16[2,1024,256]{2,1,0:T(8,128)(2,1)}, bf16[2,1024,256]{2,1,0:T(8,128)(2,1)}, u32[]{:S(2)}, u32[]{:S(2)}) collective-permute-start(bf16[2,1024,256]{2,1,0:T(8,128)(2,1)} %pad_maximum_fusion), channel_id=1, source_target_pairs={{0,16},{8,24},{16,32},{24,40},{32,48},{40,56},{48,64},{56,72},{64,... | collective-permute-start | bytes 3145736 | tf_op jit(solution)/shard_map/ppermute | solution.py:19
  60.1 2.7 collective-permute-start.3
  62.8 2.2 collective-permute-start.2
  70.3 93.7 %collective-permute-done = bf16[2,1024,256]{2,1,0:T(8,128)(2,1)} collective-permute-done((bf16[2,1024,256]{2,1,0:T(8,128)(2,1)}, bf16[2,1024,256]{2,1,0:T(8,128)(2,1)}, u32[]{:S(2)}, u32[]{:S(2)}) %collective-permute-start) | collective-permute-done | bytes 1048608 | tf_op jit(solution)/shard_map/ppermute | solution.py:19
  165.3 2.8 collective-permute-done.1
  171.9 1.5 copy-done.1
  173.4 1.5 copy-done
  174.9 51.1 %shard_map.101 = (f32[1024,256]{1,0:T(8,128)}, f32[2,1024,128]{2,1,0:T(8,128)}, f32[2,1024,128]{2,1,0:T(8,128)}) custom-call(s32[5]{0:T(128)} %convert_element_type.34.flag_ref, bf16[1024,256]{1,0:T(8,128)(2,1)} %q_ref.3, bf16[5,1024,256]{2,1,0:T(8,128)(2,1)} %copy-done, bf16[5,1024,256]{2,1,0:T(8,128)(2,1)} %copy-done.1), custom_call_target="tpu_custom_call" | custom-call | tf_op jit(solution)/shard_map/pallas_call | solution.py:118
  227.3 2.2 broadcast_in_dim.25
  229.5 4.9 %all-to-all-start = ((bf16[8,1024,256]{2,1,0:T(8,128)(2,1)}), bf16[8,1024,256]{2,1,0:T(8,128)(2,1)}, u32[]{:S(2)}, u32[]{:S(2)}) async-start(bf16[8,1024,256]{2,1,0:T(8,128)(2,1)} %broadcast_in_dim.25), calls=%async_computation | async-start | bytes 8388608 | tf_op jit(solution)/shard_map/all_to_all | solution.py:25
  234.4 5.8 %convolution_convert_fusion = bf16[256,4096]{1,0:T(8,128)(2,1)S(1)} fusion(bf16[1024,256]{1,0:T(8,128)(2,1)S(1)} %convert_element_type.35, bf16[1024,4096]{0,1:T(8,128)(2,1)} %bitcast.11), kind=kOutput, calls=%fused_computation | convolution fusion | flops 2148532224 | bytes 11010048 | tf_op jit(solution)/shard_map/dot_general | solution.py:198
  240.2 1.5 copy.20
  242.5 6.6 %convolution_convert_fusion.1.g_ref = bf16[1024,256]{1,0:T(8,128)(2,1)} fusion(bf16[1024,4096]{0,1:T(8,128)(2,1)} %bitcast.11, bf16[256,4096]{1,0:T(8,128)(2,1)S(1)} %copy-done.3), kind=kOutput, calls=%fused_computation.7 | convolution fusion | flops 2147745792 | bytes 11010048 | tf_op jit(solution)/shard_map/dot_general | solution.py:195
  249.1 45.8 %shard_map.102 = (f32[1024,256]{1,0:T(8,128)}, f32[5,1024,256]{2,1,0:T(8,128)}, f32[5,1024,256]{2,1,0:T(8,128)}) custom-call(s32[5]{0:T(128)} %convert_element_type.34.flag_ref, bf16[1024,256]{1,0:T(8,128)(2,1)} %q_ref.3, bf16[5,1024,256]{2,1,0:T(8,128)(2,1)} %copy-done, bf16[5,1024,256]{2,1,0:T(8,128)(2,1)} %copy-done.1, ...), custom_call_target="tpu_custom_call" | custom-call | tf_op jit(solution)/shard_map/pallas_call | solution.py:149
  294.9 2.9 convert.20
  301.5 16.8 %all-to-all-start.3 = ((bf16[256,16,256]{2,0,1:T(8,128)(2,1)}), bf16[256,16,256]{2,0,1:T(8,128)(2,1)S(1)}, u32[]{:S(2)}, u32[]{:S(2)}) async-start(bf16[256,16,256]{2,0,1:T(8,128)(2,1)} %bitcast.35), calls=%async_computation.3 | async-start | bytes 4194304 | tf_op jit(solution)/shard_map/all_to_all | solution.py:33
  319.7 2.5 collective-permute-start.5
  323.5 2.1 collective-permute-start.6
  327.2 4.2 collective-permute-start.4
  331.4 5.5 %bitcast_convert_fusion = bf16[1024,512]{1,0:T(8,128)(2,1)} fusion(bf16[256,8,512]{2,0,1:T(8,128)(2,1)S(1)} %copy-done.5, bf16[8,1024,256]{2,1,0:T(8,128)(2,1)} %all-to-all-done), kind=kOutput, calls=%fused_computation.5 | convolution fusion | flops 2148007936 | bytes 7340032 | tf_op jit(solution)/shard_map/dot_general | solution.py:192
  336.9 29.2 %collective-permute-done.5 = bf16[2,1024,256]{2,1,0:T(8,128)(2,1)S(1)} collective-permute-done((bf16[2,1024,256]{2,1,0:T(8,128)(2,1)S(1)}, bf16[2,1024,256]{2,1,0:T(8,128)(2,1)S(1)}, u32[]{:S(2)}, u32[]{:S(2)}) %collective-permute-start.5) | collective-permute-done | bytes 1048608 | tf_op jit(solution)/shard_map/ppermute | solution.py:19
  366.2 33.4 %collective-permute-done.6 = bf16[2,1024,256]{2,1,0:T(8,128)(2,1)S(1)} collective-permute-done((bf16[2,1024,256]{2,1,0:T(8,128)(2,1)S(1)}, bf16[2,1024,256]{2,1,0:T(8,128)(2,1)S(1)}, u32[]{:S(2)}, u32[]{:S(2)}) %collective-permute-start.6) | collective-permute-done | bytes 1048608 | tf_op jit(solution)/shard_map/ppermute | solution.py:19
  399.7 23.0 %collective-permute-done.7 = bf16[2,1024,256]{2,1,0:T(8,128)(2,1)S(1)} collective-permute-done((bf16[2,1024,256]{2,1,0:T(8,128)(2,1)S(1)}, bf16[2,1024,256]{2,1,0:T(8,128)(2,1)S(1)}, u32[]{:S(2)}, u32[]{:S(2)}) %collective-permute-start.7) | collective-permute-done | bytes 1048608 | tf_op jit(solution)/shard_map/ppermute | solution.py:19
  423.1 3.7 fusion.7
  (51 shorter events, 20.5 us)
Async XLA Ops:
  6.3 35.1 %all-to-all-start.1 = ((bf16[256,8,512]{2,0,1:T(8,128)(2,1)}), bf16[256,8,512]{2,0,1:T(8,128)(2,1)S(1)}, u32[]{:S(2)}, u32[]{:S(2)}) async-start(bf16[256,8,512]{2,0,1:T(8,128)(2,1)} %copy.15), calls=%async_computation.1 | async-start | bytes 4194304 | tf_op jit(solution)/shard_map/all_to_all | solution.py:191
  41.4 4.3 %copy-start.4 = (bf16[256,8,512]{2,0,1:T(8,128)(2,1)}, bf16[256,8,512]{2,0,1:T(8,128)(2,1)S(1)}, u32[]{:S(2)}) copy-start(bf16[256,8,512]{2,0,1:T(8,128)(2,1)S(1)} %all-to-all-done.1) | copy-start | bytes 6291460
  45.8 6.9 %copy-start.6 = (bf16[1024,256]{1,0:T(8,128)(2,1)S(1)}, bf16[1024,256]{1,0:T(8,128)(2,1)}, u32[]{:S(2)}) copy-start(bf16[1024,256]{1,0:T(8,128)(2,1)} %param.7) | copy-start | bytes 1572868
  45.8 6.9 %copy-start.7 = (bf16[1024,256]{1,0:T(8,128)(2,1)S(1)}, bf16[1024,256]{1,0:T(8,128)(2,1)}, u32[]{:S(2)}) copy-start(bf16[1024,256]{1,0:T(8,128)(2,1)} %param.8) | copy-start | bytes 1572868
  45.8 19.3 %copy-start.10 = (s32[16,16]{1,0:T(8,128)S(1)}, s32[16,16]{1,0:T(8,128)}, u32[]{:S(2)}) copy-start(s32[16,16]{1,0:T(8,128)} %param.11) | copy-start | bytes 3076
  45.8 181.5 %all-to-all-start.2 = ((bf16[8,1024,512]{1,2,0:T(8,128)(2,1)}), bf16[8,1024,512]{1,2,0:T(8,128)(2,1)}, u32[]{:S(2)}, u32[]{:S(2)}) async-start(bf16[8,1024,512]{1,2,0:T(8,128)(2,1)} %broadcast_in_dim.26), calls=%async_computation.2 | async-start | bytes 16777216 | tf_op jit(solution)/shard_map/all_to_all | solution.py:25
  53.7 110.3 %collective-permute-start = (bf16[2,1024,256]{2,1,0:T(8,128)(2,1)}, bf16[2,1024,256]{2,1,0:T(8,128)(2,1)}, u32[]{:S(2)}, u32[]{:S(2)}) collective-permute-start(bf16[2,1024,256]{2,1,0:T(8,128)(2,1)} %pad_maximum_fusion), channel_id=1, source_target_pairs={{0,8},{8,16},{16,24},{24,32},{32,40},{40,48},{48,56},{56,64},{64,7... | collective-permute-start | bytes 3145736 | tf_op jit(solution)/shard_map/ppermute | solution.py:19
  55.6 112.4 %collective-permute-start.1 = (bf16[2,1024,256]{2,1,0:T(8,128)(2,1)}, bf16[2,1024,256]{2,1,0:T(8,128)(2,1)}, u32[]{:S(2)}, u32[]{:S(2)}) collective-permute-start(bf16[2,1024,256]{2,1,0:T(8,128)(2,1)} %pad_maximum_fusion), channel_id=1, source_target_pairs={{0,16},{8,24},{16,32},{24,40},{32,48},{40,56},{48,64},{56,72},{64,... | collective-permute-start | bytes 3145736 | tf_op jit(solution)/shard_map/ppermute | solution.py:19
  60.1 110.5 %collective-permute-start.3 = (bf16[2,1024,256]{2,1,0:T(8,128)(2,1)}, bf16[2,1024,256]{2,1,0:T(8,128)(2,1)}, u32[]{:S(2)}, u32[]{:S(2)}) collective-permute-start(bf16[2,1024,256]{2,1,0:T(8,128)(2,1)} %pad_maximum_fusion), channel_id=1, source_target_pairs={{0,64},{8,72},{16,80},{24,88},{32,96},{40,104},{48,112},{56,120},{... | collective-permute-start | bytes 3145736 | tf_op jit(solution)/shard_map/ppermute | solution.py:19
  62.8 106.5 %collective-permute-start.2 = (bf16[2,1024,256]{2,1,0:T(8,128)(2,1)}, bf16[2,1024,256]{2,1,0:T(8,128)(2,1)}, u32[]{:S(2)}, u32[]{:S(2)}) collective-permute-start(bf16[2,1024,256]{2,1,0:T(8,128)(2,1)} %pad_maximum_fusion), channel_id=1, source_target_pairs={{0,32},{8,40},{16,48},{24,56},{32,64},{40,72},{48,80},{56,88},{64,... | collective-permute-start | bytes 3145736 | tf_op jit(solution)/shard_map/ppermute | solution.py:19
  171.9 1.5 copy-start.1
  173.4 1.5 copy-start
  229.5 72.0 %all-to-all-start = ((bf16[8,1024,256]{2,1,0:T(8,128)(2,1)}), bf16[8,1024,256]{2,1,0:T(8,128)(2,1)}, u32[]{:S(2)}, u32[]{:S(2)}) async-start(bf16[8,1024,256]{2,1,0:T(8,128)(2,1)} %broadcast_in_dim.25), calls=%async_computation | async-start | bytes 8388608 | tf_op jit(solution)/shard_map/all_to_all | solution.py:25
  240.2 2.4 copy-start.3
  294.9 4.0 copy-start.2
  301.5 125.3 %all-to-all-start.3 = ((bf16[256,16,256]{2,0,1:T(8,128)(2,1)}), bf16[256,16,256]{2,0,1:T(8,128)(2,1)S(1)}, u32[]{:S(2)}, u32[]{:S(2)}) async-start(bf16[256,16,256]{2,0,1:T(8,128)(2,1)} %bitcast.35), calls=%async_computation.3 | async-start | bytes 4194304 | tf_op jit(solution)/shard_map/all_to_all | solution.py:33
  318.3 7.3 %copy-start.8 = (bf16[1,1024,256]{2,1,0:T(8,128)(2,1)S(1)}, bf16[1,1024,256]{2,1,0:T(8,128)(2,1)}, u32[]{:S(2)}) copy-start(bf16[1,1024,256]{2,1,0:T(8,128)(2,1)} %get-tuple-element.24) | copy-start | bytes 1572868
  318.3 7.4 %copy-start.9 = (bf16[1,1024,256]{2,1,0:T(8,128)(2,1)S(1)}, bf16[1,1024,256]{2,1,0:T(8,128)(2,1)}, u32[]{:S(2)}) copy-start(bf16[1,1024,256]{2,1,0:T(8,128)(2,1)} %get-tuple-element.28) | copy-start | bytes 1572868
  319.7 46.4 %collective-permute-start.5 = (bf16[2,1024,256]{2,1,0:T(8,128)(2,1)S(1)}, bf16[2,1024,256]{2,1,0:T(8,128)(2,1)S(1)}, u32[]{:S(2)}, u32[]{:S(2)}) collective-permute-start(bf16[2,1024,256]{2,1,0:T(8,128)(2,1)S(1)} %pad_maximum_fusion.2), channel_id=1, source_target_pairs={{16,0},{24,8},{32,16},{40,24},{48,32},{56,40},{64,48},{72,56},{80,... | collective-permute-start | bytes 3145736 | tf_op jit(solution)/shard_map/ppermute | solution.py:19
  323.5 7.9 %copy-start.5 = (bf16[256,8,512]{2,0,1:T(8,128)(2,1)S(1)}, bf16[256,8,512]{2,0,1:T(8,128)(2,1)}, u32[]{:S(2)}) copy-start(bf16[256,8,512]{2,0,1:T(8,128)(2,1)} %copy-done.4) | copy-start | bytes 6291460
  323.5 76.1 %collective-permute-start.6 = (bf16[2,1024,256]{2,1,0:T(8,128)(2,1)S(1)}, bf16[2,1024,256]{2,1,0:T(8,128)(2,1)S(1)}, u32[]{:S(2)}, u32[]{:S(2)}) collective-permute-start(bf16[2,1024,256]{2,1,0:T(8,128)(2,1)S(1)} %pad_maximum_fusion.3), channel_id=1, source_target_pairs={{32,0},{40,8},{48,16},{56,24},{64,32},{72,40},{80,48},{88,56},{96,... | collective-permute-start | bytes 3145736 | tf_op jit(solution)/shard_map/ppermute | solution.py:19
  325.7 97.0 %collective-permute-start.7 = (bf16[2,1024,256]{2,1,0:T(8,128)(2,1)S(1)}, bf16[2,1024,256]{2,1,0:T(8,128)(2,1)S(1)}, u32[]{:S(2)}, u32[]{:S(2)}) collective-permute-start(bf16[2,1024,256]{2,1,0:T(8,128)(2,1)S(1)} %pad_maximum_fusion.4), channel_id=1, source_target_pairs={{64,0},{72,8},{80,16},{88,24},{96,32},{104,40},{112,48},{120,56},{... | collective-permute-start | bytes 3145736 | tf_op jit(solution)/shard_map/ppermute | solution.py:19
  327.2 95.7 %collective-permute-start.4 = (bf16[2,1024,256]{2,1,0:T(8,128)(2,1)S(1)}, bf16[2,1024,256]{2,1,0:T(8,128)(2,1)S(1)}, u32[]{:S(2)}, u32[]{:S(2)}) collective-permute-start(bf16[2,1024,256]{2,1,0:T(8,128)(2,1)S(1)} %pad_maximum_fusion.1), channel_id=1, source_target_pairs={{8,0},{16,8},{24,16},{32,24},{40,32},{48,40},{56,48},{64,56},{72,6... | collective-permute-start | bytes 3145736 | tf_op jit(solution)/shard_map/ppermute | solution.py:19
where the time goes:
time: 429 us; the launch traced here: 428 us
  waiting for transfers between devices  210 us (49%)
  Pallas kernels  96.8 us (23%)
  starting transfers between devices  55.6 us (13%)
  local copies, waits for them, and re-layouts  29.1 us (7%)
  matrix products  17.8 us (4%)
  other arithmetic  15 us (3%)
    ppermute x8, waiting for transfers between devices, passed_along(): lax.ppermute(value, axis, [(source, source + steps) for source in range(i...  182 us
    pallas_call x1, Pallas kernels, attention_forward(): pl.pallas_call(kernel, grid_spec=pltpu.PrefetchScalarGridSpec(num_scalar_...  51.1 us
    pallas_call x1, Pallas kernels, attention_backward(): pl.pallas_call(kernel, grid_spec=pltpu.PrefetchScalarGridSpec(num_scalar_...  45.8 us
    all_to_all x1, waiting for transfers between devices, local(): lax.all_to_all(out_weight, 'tp', split_axis=1, concat_axis=0, tiled=True)  27.8 us
    ppermute x8, starting transfers between devices, passed_along(): lax.ppermute(value, axis, [(source, source + steps) for source in range(i...  21.4 us
    all_to_all x1, starting transfers between devices, summed_scatter(): parts = lax.all_to_all(pieces, axis, 1, 1, tiled=True)  16.8 us
    unnamed x28, local copies, waits for them, and re-layouts  14.8 us
    all_to_all x2, starting transfers between devices, gathered(): parts = lax.all_to_all(spread, axis, 0, 0, tiled=True)  11.7 us
  transfers between devices with their start and end apart: 12, of which 6 were waited for; matrix products, arithmetic and copies ran while one was open for 10% of the time, Pallas kernels for 23%

commit v1 on v0

--- a/solution.py
+++ b/solution.py
@@ -186,20 +186,42 @@
         flags.append((target >= 0) & (linked == 1))
     flags = jnp.stack(flags).astype(jnp.int32)
 
+    tp_len = lax.axis_size("tp")
+    tp_index = lax.axis_index("tp")
+    weight_cols = lax.all_to_all(out_weight, "tp", split_axis=1, concat_axis=0, tiled=True)
+    grad_part = lax.dot_general(
+        cotangent, weight_cols, (((1,), (1,)), ((), ())), preferred_element_type=jnp.float32
+    )
+    grad_parts = lax.all_to_all(
+        grad_part.astype(jnp.bfloat16).reshape(block_len, tp_len, local_cols), "tp", 1, 1, tiled=True
+    )
+    grad_heads = jnp.sum(grad_parts.astype(jnp.float32), axis=1).astype(jnp.bfloat16)
+
     attended32, row_max, row_total = attention_forward(flags, queries, keys_all, values_all, score_scale)
     attended = attended32.astype(jnp.bfloat16)
-    weight_cols = lax.all_to_all(out_weight, "tp", split_axis=1, concat_axis=0, tiled=True)
-    mixed_sum = jnp.dot(gathered(attended, "tp"), weight_cols, preferred_element_type=jnp.float32)
+    spread = jnp.broadcast_to(attended[None], (tp_len,) + attended.shape)
+    att_parts = lax.all_to_all(spread, "tp", 0, 0, tiled=True)
+    mixed_sum = jnp.einsum(
+        "ktc,kcf->tf",
+        att_parts,
+        weight_cols.reshape(tp_len, local_cols, weight_cols.shape[1]),
+        preferred_element_type=jnp.float32,
+    )
     mixed = mixed_sum.astype(jnp.bfloat16)
-    piece = gathered(cotangent, "tp")
-    grad_att = lax.dot_general(
-        piece, out_weight, (((1,), (1,)), ((), ())), preferred_element_type=jnp.float32
-    )
-    weight_part = lax.dot_general(
-        attended, piece, (((0,), (0,)), ((), ())), preferred_element_type=jnp.float32
-    )
-    d_weight = summed_scatter(weight_part.astype(jnp.bfloat16), "ctx")
-    grad_heads = grad_att.astype(jnp.bfloat16)
+    weight_part = jnp.einsum("ktc,tf->kcf", att_parts, cotangent, preferred_element_type=jnp.float32)
+    halves = cotangent.shape[1] // local_cols
+    pieces = (
+        weight_part.astype(jnp.bfloat16)
+        .reshape(tp_len, local_cols, halves, local_cols)
+        .transpose(0, 2, 1, 3)
+        .reshape(tp_len * halves, local_cols, local_cols)
+    )
+    reduced = jnp.sum(lax.all_to_all(pieces, "ctx", 0, 0, tiled=True).astype(jnp.float32), axis=0)
+    moves = []
+    for k in range(axis_len):
+        for p in range(tp_len):
+            moves.append((k * tp_len + p, (halves * p + k % halves) * tp_len + k // halves))
+    d_weight = lax.ppermute(reduced, ("ctx", "tp"), moves)
     grad_query, key_grads, value_grads = attention_backward(
         flags, queries, keys_all, values_all, grad_heads, attended32, row_max, row_total, score_scale
     )

time: 429 us -> 454 us (1.058)
  the two profiles are of different devices: /device:TPU:56 before, /device:TPU:43 now
where the time goes in v1:
time: 454 us; the launch traced here: 453 us
  waiting for transfers between devices  206 us (45%)
  Pallas kernels  96.8 us (21%)
  starting transfers between devices  84.8 us (19%)
  other arithmetic  25.5 us (6%)
  local copies, waits for them, and re-layouts  21.4 us (5%)
  matrix products  14.7 us (3%)
    ppermute x8, waiting for transfers between devices, passed_along(): lax.ppermute(value, axis, [(source, source + steps) for source in range(i...  89.3 us
    pallas_call x1, Pallas kernels, attention_forward(): pl.pallas_call(kernel, grid_spec=pltpu.PrefetchScalarGridSpec(num_scalar_...  51.1 us
    all_to_all x1, waiting for transfers between devices, local(): att_parts = lax.all_to_all(spread, 'tp', 0, 0, tiled=True)  50.4 us
    all_to_all x1, waiting for transfers between devices, local(): lax.all_to_all(grad_part.astype(jnp.bfloat16).reshape(block_len, tp_len,...  48.3 us
    pallas_call x1, Pallas kernels, attention_backward(): pl.pallas_call(kernel, grid_spec=pltpu.PrefetchScalarGridSpec(num_scalar_...  45.8 us
    ppermute x1, starting transfers between devices, local(): d_weight = lax.ppermute(reduced, ('ctx', 'tp'), moves)  36.3 us
    ppermute x8, starting transfers between devices, passed_along(): lax.ppermute(value, axis, [(source, source + steps) for source in range(i...  23.6 us
    ppermute x1, waiting for transfers between devices, local(): d_weight = lax.ppermute(reduced, ('ctx', 'tp'), moves)  17.9 us
  transfers between devices with their start and end apart: 13, of which 9 were waited for; matrix products, arithmetic and copies ran while one was open for 12% of the time, Pallas kernels for 21%

profile of v1, /device:TPU:43, one launch (start us, length us, event | category | flops | bytes accessed | tf_op | source)
XLA Modules:
  0.0 452.6 jit_solution(8794539153537897448)
XLA Ops:
  0.6 2.4 pad_maximum_fusion.1
  3.0 4.5 collective-permute-start
  7.5 4.2 collective-permute-start.1
  11.7 3.3 copy.15
  15.0 2.4 copy.16
  17.4 5.3 %all-to-all-start.1 = ((bf16[256,8,512]{2,0,1:T(8,128)(2,1)}), bf16[256,8,512]{2,0,1:T(8,128)(2,1)}, u32[]{:S(2)}, u32[]{:S(2)}) async-start(bf16[256,8,512]{2,0,1:T(8,128)(2,1)} %copy.16), calls=%async_computation.1 | async-start | bytes 4194304 | tf_op jit(solution)/shard_map/all_to_all | solution.py:191
  22.7 2.5 collective-permute-start.3
  32.4 12.6 %collective-permute-done = bf16[2,1024,256]{2,1,0:T(8,128)(2,1)} collective-permute-done((bf16[2,1024,256]{2,1,0:T(8,128)(2,1)}, bf16[2,1024,256]{2,1,0:T(8,128)(2,1)}, u32[]{:S(2)}, u32[]{:S(2)}) %collective-permute-start) | collective-permute-done | bytes 1048608 | tf_op jit(solution)/shard_map/ppermute | solution.py:19
  45.0 2.3 slice_dynamic-update-slice_fusion.3
  47.3 16.7 %collective-permute-done.1 = bf16[2,1024,256]{2,1,0:T(8,128)(2,1)} collective-permute-done((bf16[2,1024,256]{2,1,0:T(8,128)(2,1)}, bf16[2,1024,256]{2,1,0:T(8,128)(2,1)}, u32[]{:S(2)}, u32[]{:S(2)}) %collective-permute-start.1) | collective-permute-done | bytes 1048608 | tf_op jit(solution)/shard_map/ppermute | solution.py:19
  64.0 2.3 slice_dynamic-update-slice_fusion.2
  66.2 25.9 %collective-permute-done.2 = bf16[2,1024,256]{2,1,0:T(8,128)(2,1)} collective-permute-done((bf16[2,1024,256]{2,1,0:T(8,128)(2,1)}, bf16[2,1024,256]{2,1,0:T(8,128)(2,1)}, u32[]{:S(2)}, u32[]{:S(2)}) %collective-permute-start.2) | collective-permute-done | bytes 1048608 | tf_op jit(solution)/shard_map/ppermute | solution.py:19
  95.4 51.1 %shard_map.101 = (f32[1024,256]{1,0:T(8,128)}, f32[2,1024,128]{2,1,0:T(8,128)}, f32[2,1024,128]{2,1,0:T(8,128)}) custom-call(s32[5]{0:T(128)} %convert_element_type.36.flag_ref, bf16[1024,256]{1,0:T(8,128)(2,1)} %q_ref.3, bf16[5,1024,256]{2,1,0:T(8,128)(2,1)} %get-tuple-element.34.k_ref, bf16[5,1024,256]{2,1,0:T(8,128)(2,1)} %get-tuple-element.33.v_ref), custom_call_target="tpu_custom_call" | custom-call | tf_op jit(solution)/shard_map/pallas_call | solution.py:118
  150.0 6.6 %all-to-all-start = ((bf16[8,1024,256]{2,1,0:T(8,128)(2,1)}), bf16[8,1024,256]{2,1,0:T(8,128)(2,1)}, u32[]{:S(2)}, u32[]{:S(2)}) async-start(bf16[8,1024,256]{2,1,0:T(8,128)(2,1)} %broadcast_in_dim.19), calls=%async_computation | async-start | bytes 8388608 | tf_op jit(solution)/shard_map/all_to_all | solution.py:203
  156.6 4.0 convolution_convert_fusion
  160.6 2.3 copy.22
  162.8 50.4 %all-to-all-done = bf16[8,1024,256]{2,1,0:T(8,128)(2,1)} async-done(((bf16[8,1024,256]{2,1,0:T(8,128)(2,1)}), bf16[8,1024,256]{2,1,0:T(8,128)(2,1)}, u32[]{:S(2)}, u32[]{:S(2)}) %all-to-all-start) | async-done | bytes 4194336 | tf_op jit(solution)/shard_map/all_to_all | solution.py:203
  213.3 7.1 %all-to-all-start.2 = ((bf16[1024,8,256]{2,0,1:T(8,128)(2,1)}), bf16[1024,8,256]{2,0,1:T(8,128)(2,1)}, u32[]{:S(2)}, u32[]{:S(2)}) async-start(bf16[1024,8,256]{2,0,1:T(8,128)(2,1)} %bitcast.34), calls=%async_computation.2 | async-start | bytes 8388608 | tf_op jit(solution)/shard_map/all_to_all | solution.py:195
  220.4 4.6 %convolution_convert_fusion.1 = bf16[8,256,512]{2,1,0:T(8,128)(2,1)S(1)} fusion(bf16[8,1024,256]{2,1,0:T(8,128)(2,1)} %all-to-all-done, bf16[1024,512]{1,0:T(8,128)(2,1)S(1)} %copy-done), kind=kOutput, calls=%fused_computation.7 | convolution fusion | flops 2148532224 | bytes 7340032 | tf_op jit(solution)/shard_map/ktc,tf->kcf/dot_general | solution.py:211
  226.6 48.3 %all-to-all-done.2 = bf16[1024,8,256]{2,0,1:T(8,128)(2,1)} async-done(((bf16[1024,8,256]{2,0,1:T(8,128)(2,1)}), bf16[1024,8,256]{2,0,1:T(8,128)(2,1)}, u32[]{:S(2)}, u32[]{:S(2)}) %all-to-all-start.2) | async-done | bytes 4194336 | tf_op jit(solution)/shard_map/all_to_all | solution.py:195
  274.9 5.8 %all-to-all-start.3 = ((bf16[16,256,256]{2,1,0:T(8,128)(2,1)}), bf16[16,256,256]{2,1,0:T(8,128)(2,1)S(1)}, u32[]{:S(2)}, u32[]{:S(2)}) async-start(bf16[16,256,256]{2,1,0:T(8,128)(2,1)} %bitcast.13), calls=%async_computation.3 | async-start | bytes 4194304 | tf_op jit(solution)/shard_map/all_to_all | solution.py:219
  280.8 3.7 reduce_sum.71.g_ref
  284.5 45.8 %shard_map.102 = (f32[1024,256]{1,0:T(8,128)}, f32[5,1024,256]{2,1,0:T(8,128)}, f32[5,1024,256]{2,1,0:T(8,128)}) custom-call(s32[5]{0:T(128)} %convert_element_type.36.flag_ref, bf16[1024,256]{1,0:T(8,128)(2,1)} %q_ref.3, bf16[5,1024,256]{2,1,0:T(8,128)(2,1)} %get-tuple-element.34.k_ref, bf16[5,1024,256]{2,1,0:T(8,128)(2,1)} %get-tuple-element.33.v_ref, ...), custom_call_target="tpu_custom_call" | custom-call | tf_op jit(solution)/shard_map/pallas_call | solution.py:149
  330.3 2.9 convert.21
  334.8 4.6 %collective-permute-start.5 = (bf16[2,1024,256]{2,1,0:T(8,128)(2,1)S(1)}, bf16[2,1024,256]{2,1,0:T(8,128)(2,1)S(1)}, u32[]{:S(2)}, u32[]{:S(2)}) collective-permute-start(bf16[2,1024,256]{2,1,0:T(8,128)(2,1)S(1)} %pad_maximum_fusion.3), channel_id=1, source_target_pairs={{16,0},{24,8},{32,16},{40,24},{48,32},{56,40},{64,48},{72,56},{80,... | collective-permute-start | bytes 3145736 | tf_op jit(solution)/shard_map/ppermute | solution.py:19
  342.9 2.6 collective-permute-start.4
  345.5 6.2 %bitcast_convert_fusion = bf16[1024,512]{1,0:T(8,128)(2,1)} fusion(bf16[8,1024,256]{2,1,0:T(8,128)(2,1)} %all-to-all-done, bf16[256,8,512]{2,0,1:T(8,128)(2,1)} %all-to-all-done.1), kind=kOutput, calls=%fused_computation.4 | convolution fusion | flops 2148007936 | bytes 7340032 | tf_op jit(solution)/shard_map/ktc,kcf->tf/dot_general | solution.py:204
  351.7 10.9 %collective-permute-done.5 = bf16[2,1024,256]{2,1,0:T(8,128)(2,1)S(1)} collective-permute-done((bf16[2,1024,256]{2,1,0:T(8,128)(2,1)S(1)}, bf16[2,1024,256]{2,1,0:T(8,128)(2,1)S(1)}, u32[]{:S(2)}, u32[]{:S(2)}) %collective-permute-start.5) | collective-permute-done | bytes 1048608 | tf_op jit(solution)/shard_map/ppermute | solution.py:19
  366.9 21.9 %collective-permute-done.7 = bf16[2,1024,256]{2,1,0:T(8,128)(2,1)S(1)} collective-permute-done((bf16[2,1024,256]{2,1,0:T(8,128)(2,1)S(1)}, bf16[2,1024,256]{2,1,0:T(8,128)(2,1)S(1)}, u32[]{:S(2)}, u32[]{:S(2)}) %collective-permute-start.7) | collective-permute-done | bytes 1048608 | tf_op jit(solution)/shard_map/ppermute | solution.py:19
  392.1 36.3 %collective-permute-start.8 = (f32[256,256]{1,0:T(8,128)S(1)}, f32[256,256]{1,0:T(8,128)S(1)}, u32[]{:S(2)}, u32[]{:S(2)}) collective-permute-start(f32[256,256]{1,0:T(8,128)S(1)} %convert_reduce_fusion), channel_id=1, source_target_pairs={{0,0},{1,16},{2,32},{3,48},{4,64},{5,80},{6,96},{7,112},{8,8},{9,2... | collective-permute-start | bytes 786440 | tf_op jit(solution)/shard_map/ppermute | solution.py:224
  428.4 5.6 %fusion.4 = (f32[1024,256]{1,0:T(8,128)}, f32[1024,256]{1,0:T(8,128)}) fusion(f32[2,1024,256]{2,1,0:T(8,128)} %convert_element_type.43, f32[2,1024,256]{2,1,0:T(8,128)} %convert_element_type.42, f32[2,1024,256]{2,1,0:T(8,128)S(1)} %copy-done.2, f32[2,1024,256]{2,1,0:T(8,128)} %convert_element_type.40, f32[5,1024,256]{2,1,0:T(8,128)} %get-tuple-element.16, ...), kind=kLoop, calls=%fused_computation.9 | loop fusion | flops 2097152 | bytes 12582912 | tf_op jit(solution)/shard_map/add | solution.py:234
  434.0 17.9 %collective-permute-done.8 = f32[256,256]{1,0:T(8,128)S(1)} collective-permute-done((f32[256,256]{1,0:T(8,128)S(1)}, f32[256,256]{1,0:T(8,128)S(1)}, u32[]{:S(2)}, u32[]{:S(2)}) %collective-permute-start.8) | collective-permute-done | bytes 262176 | tf_op jit(solution)/shard_map/ppermute | solution.py:224
  (50 shorter events, 26.5 us)
Async XLA Ops:
  0.6 156.0 %copy-start = (bf16[1024,512]{1,0:T(8,128)(2,1)S(1)}, bf16[1024,512]{1,0:T(8,128)(2,1)}, u32[]{:S(2)}) copy-start(bf16[1024,512]{1,0:T(8,128)(2,1)} %param.10) | copy-start | bytes 3145732
  3.0 42.0 %collective-permute-start = (bf16[2,1024,256]{2,1,0:T(8,128)(2,1)}, bf16[2,1024,256]{2,1,0:T(8,128)(2,1)}, u32[]{:S(2)}, u32[]{:S(2)}) collective-permute-start(bf16[2,1024,256]{2,1,0:T(8,128)(2,1)} %pad_maximum_fusion.1), channel_id=1, source_target_pairs={{0,8},{8,16},{16,24},{24,32},{32,40},{40,48},{48,56},{56,64},{64,7... | collective-permute-start | bytes 3145736 | tf_op jit(solution)/shard_map/ppermute | solution.py:19
  7.5 56.5 %collective-permute-start.1 = (bf16[2,1024,256]{2,1,0:T(8,128)(2,1)}, bf16[2,1024,256]{2,1,0:T(8,128)(2,1)}, u32[]{:S(2)}, u32[]{:S(2)}) collective-permute-start(bf16[2,1024,256]{2,1,0:T(8,128)(2,1)} %pad_maximum_fusion.1), channel_id=1, source_target_pairs={{0,16},{8,24},{16,32},{24,40},{32,48},{40,56},{48,64},{56,72},{64,... | collective-permute-start | bytes 3145736 | tf_op jit(solution)/shard_map/ppermute | solution.py:19
  17.4 9.9 %copy-start.5 = (s32[16,16]{1,0:T(8,128)S(1)}, s32[16,16]{1,0:T(8,128)}, u32[]{:S(2)}) copy-start(s32[16,16]{1,0:T(8,128)} %param.11) | copy-start | bytes 3076
  17.4 13.9 %copy-start.3 = (bf16[1024,256]{1,0:T(8,128)(2,1)S(1)}, bf16[1024,256]{1,0:T(8,128)(2,1)}, u32[]{:S(2)}) copy-start(bf16[1024,256]{1,0:T(8,128)(2,1)} %param.7) | copy-start | bytes 1572868
  17.4 13.9 %copy-start.4 = (bf16[1024,256]{1,0:T(8,128)(2,1)S(1)}, bf16[1024,256]{1,0:T(8,128)(2,1)}, u32[]{:S(2)}) copy-start(bf16[1024,256]{1,0:T(8,128)(2,1)} %param.8) | copy-start | bytes 1572868
  17.4 130.3 %all-to-all-start.1 = ((bf16[256,8,512]{2,0,1:T(8,128)(2,1)}), bf16[256,8,512]{2,0,1:T(8,128)(2,1)}, u32[]{:S(2)}, u32[]{:S(2)}) async-start(bf16[256,8,512]{2,0,1:T(8,128)(2,1)} %copy.16), calls=%async_computation.1 | async-start | bytes 4194304 | tf_op jit(solution)/shard_map/all_to_all | solution.py:191
  22.7 71.6 %collective-permute-start.3 = (bf16[2,1024,256]{2,1,0:T(8,128)(2,1)}, bf16[2,1024,256]{2,1,0:T(8,128)(2,1)S(1)}, u32[]{:S(2)}, u32[]{:S(2)}) collective-permute-start(bf16[2,1024,256]{2,1,0:T(8,128)(2,1)} %pad_maximum_fusion.1), channel_id=1, source_target_pairs={{0,64},{8,72},{16,80},{24,88},{32,96},{40,104},{48,112},{56,120},{... | collective-permute-start | bytes 3145736 | tf_op jit(solution)/shard_map/ppermute | solution.py:19
  25.2 66.9 %collective-permute-start.2 = (bf16[2,1024,256]{2,1,0:T(8,128)(2,1)}, bf16[2,1024,256]{2,1,0:T(8,128)(2,1)}, u32[]{:S(2)}, u32[]{:S(2)}) collective-permute-start(bf16[2,1024,256]{2,1,0:T(8,128)(2,1)} %pad_maximum_fusion.1), channel_id=1, source_target_pairs={{0,32},{8,40},{16,48},{24,56},{32,64},{40,72},{48,80},{56,88},{64,... | collective-permute-start | bytes 3145736 | tf_op jit(solution)/shard_map/ppermute | solution.py:19
  150.0 63.3 %all-to-all-start = ((bf16[8,1024,256]{2,1,0:T(8,128)(2,1)}), bf16[8,1024,256]{2,1,0:T(8,128)(2,1)}, u32[]{:S(2)}, u32[]{:S(2)}) async-start(bf16[8,1024,256]{2,1,0:T(8,128)(2,1)} %broadcast_in_dim.19), calls=%async_computation | async-start | bytes 8388608 | tf_op jit(solution)/shard_map/all_to_all | solution.py:203
  213.3 61.7 %all-to-all-start.2 = ((bf16[1024,8,256]{2,0,1:T(8,128)(2,1)}), bf16[1024,8,256]{2,0,1:T(8,128)(2,1)}, u32[]{:S(2)}, u32[]{:S(2)}) async-start(bf16[1024,8,256]{2,0,1:T(8,128)(2,1)} %bitcast.34), calls=%async_computation.2 | async-start | bytes 8388608 | tf_op jit(solution)/shard_map/all_to_all | solution.py:195
  274.9 116.8 %all-to-all-start.3 = ((bf16[16,256,256]{2,1,0:T(8,128)(2,1)}), bf16[16,256,256]{2,1,0:T(8,128)(2,1)S(1)}, u32[]{:S(2)}, u32[]{:S(2)}) async-start(bf16[16,256,256]{2,1,0:T(8,128)(2,1)} %bitcast.13), calls=%async_computation.3 | async-start | bytes 4194304 | tf_op jit(solution)/shard_map/all_to_all | solution.py:219
  330.3 3.7 slice-start
  330.3 4.0 slice-start.1
  334.8 27.7 %collective-permute-start.5 = (bf16[2,1024,256]{2,1,0:T(8,128)(2,1)S(1)}, bf16[2,1024,256]{2,1,0:T(8,128)(2,1)S(1)}, u32[]{:S(2)}, u32[]{:S(2)}) collective-permute-start(bf16[2,1024,256]{2,1,0:T(8,128)(2,1)S(1)} %pad_maximum_fusion.3), channel_id=1, source_target_pairs={{16,0},{24,8},{32,16},{40,24},{48,32},{56,40},{64,48},{72,56},{80,... | collective-permute-start | bytes 3145736 | tf_op jit(solution)/shard_map/ppermute | solution.py:19
  339.5 25.9 %collective-permute-start.6 = (bf16[2,1024,256]{2,1,0:T(8,128)(2,1)S(1)}, bf16[2,1024,256]{2,1,0:T(8,128)(2,1)S(1)}, u32[]{:S(2)}, u32[]{:S(2)}) collective-permute-start(bf16[2,1024,256]{2,1,0:T(8,128)(2,1)S(1)} %pad_maximum_fusion.4), channel_id=1, source_target_pairs={{32,0},{40,8},{48,16},{56,24},{64,32},{72,40},{80,48},{88,56},{96,... | collective-permute-start | bytes 3145736 | tf_op jit(solution)/shard_map/ppermute | solution.py:19
  341.5 47.3 %collective-permute-start.7 = (bf16[2,1024,256]{2,1,0:T(8,128)(2,1)S(1)}, bf16[2,1024,256]{2,1,0:T(8,128)(2,1)S(1)}, u32[]{:S(2)}, u32[]{:S(2)}) collective-permute-start(bf16[2,1024,256]{2,1,0:T(8,128)(2,1)S(1)} %pad_maximum_fusion.5), channel_id=1, source_target_pairs={{64,0},{72,8},{80,16},{88,24},{96,32},{104,40},{112,48},{120,56},{... | collective-permute-start | bytes 3145736 | tf_op jit(solution)/shard_map/ppermute | solution.py:19
  342.9 47.4 %collective-permute-start.4 = (bf16[2,1024,256]{2,1,0:T(8,128)(2,1)S(1)}, bf16[2,1024,256]{2,1,0:T(8,128)(2,1)S(1)}, u32[]{:S(2)}, u32[]{:S(2)}) collective-permute-start(bf16[2,1024,256]{2,1,0:T(8,128)(2,1)S(1)} %pad_maximum_fusion.2), channel_id=1, source_target_pairs={{8,0},{16,8},{24,16},{32,24},{40,32},{48,40},{56,48},{64,56},{72,6... | collective-permute-start | bytes 3145736 | tf_op jit(solution)/shard_map/ppermute | solution.py:19
  391.8 36.6 %copy-start.2 = (f32[2,1024,256]{2,1,0:T(8,128)S(1)}, f32[2,1024,256]{2,1,0:T(8,128)}, u32[]{:S(2)}) copy-start(f32[2,1024,256]{2,1,0:T(8,128)} %convert_element_type.41) | copy-start | bytes 6291460
  392.1 59.8 %collective-permute-start.8 = (f32[256,256]{1,0:T(8,128)S(1)}, f32[256,256]{1,0:T(8,128)S(1)}, u32[]{:S(2)}, u32[]{:S(2)}) collective-permute-start(f32[256,256]{1,0:T(8,128)S(1)} %convert_reduce_fusion), channel_id=1, source_target_pairs={{0,0},{1,16},{2,32},{3,48},{4,64},{5,80},{6,96},{7,112},{8,8},{9,2... | collective-permute-start | bytes 786440 | tf_op jit(solution)/shard_map/ppermute | solution.py:224
  428.4 24.2 %copy-start.1 = (bf16[1024,512]{1,0:T(8,128)(2,1)S(1)}, bf16[1024,512]{1,0:T(8,128)(2,1)}, u32[]{:S(2)}) copy-start(bf16[1024,512]{1,0:T(8,128)(2,1)} %param.10) | copy-start | bytes 3145732

commit v2 on v1

--- a/solution.py
+++ b/solution.py
@@ -17,21 +17,6 @@
     count = lax.axis_size(axis)
     initial, last = (max(0, -steps), min(count, count - steps))
     return lax.ppermute(value, axis, [(source, source + steps) for source in range(initial, last)])
-
-
-def gathered(piece, axis):
-    count = lax.axis_size(axis)
-    spread = jnp.broadcast_to(piece[None], (count,) + piece.shape)
-    parts = lax.all_to_all(spread, axis, 0, 0, tiled=True)
-    return jnp.moveaxis(parts, 0, 1).reshape(piece.shape[0], count * piece.shape[1])
-
-
-def summed_scatter(part, axis):
-    count = lax.axis_size(axis)
-    rows, cols = part.shape
-    pieces = part.reshape(rows, count, cols // count)
-    parts = lax.all_to_all(pieces, axis, 1, 1, tiled=True)
-    return jnp.sum(parts.astype(jnp.float32), axis=1)
 
 
 def masked_scores(flag_ref, q, k, step, tiles, scale):
@@ -45,7 +30,7 @@
     return jnp.where(rows + offset >= cols, raw, NEG)
 
 
-def forward_kernel(flag_ref, q_ref, k_ref, v_ref, att_ref, m_ref, l_ref, m_sc, l_sc, acc_sc, *, tiles, steps, scale):
+def forward_kernel(flag_ref, q_ref, k_ref, v_ref, after_ref, att_ref, m_ref, l_ref, m_sc, l_sc, acc_sc, *, tiles, steps, scale):
     phase = pl.program_id(1)
     step = pl.program_id(2)
     scores = masked_scores(flag_ref, q_ref[...], k_ref[...], step, tiles, scale)
@@ -105,7 +90,7 @@
         dq_ref[...] = dq_sc[...]
 
 
-def attention_forward(flags, queries, keys_all, values_all, scale):
+def attention_forward(flags, queries, keys_all, values_all, after, scale):
     nblocks, block_len, cols = keys_all.shape
     heads = cols // DH
     tiles = block_len // KEY_TILE
@@ -120,7 +105,7 @@
         grid_spec=pltpu.PrefetchScalarGridSpec(
             num_scalar_prefetch=1,
             grid=(heads, 2, steps),
-            in_specs=[q_spec, k_spec, v_spec],
+            in_specs=[q_spec, k_spec, v_spec, pl.BlockSpec(memory_space=pl.ANY)],
             out_specs=[q_spec, stat_spec, stat_spec],
             scratch_shapes=[
                 pltpu.VMEM((block_len, 1), jnp.float32),
@@ -134,7 +119,7 @@
             jax.ShapeDtypeStruct((heads, block_len, DH), jnp.float32),
         ],
         compiler_params=pltpu.CompilerParams(dimension_semantics=("arbitrary", "arbitrary", "arbitrary")),
-    )(flags, queries, keys_all, values_all)
+    )(flags, queries, keys_all, values_all, after)
 
 
 def attention_backward(flags, queries, keys_all, values_all, grads, attended32, row_max, row_total, scale):
@@ -197,7 +182,9 @@
     )
     grad_heads = jnp.sum(grad_parts.astype(jnp.float32), axis=1).astype(jnp.bfloat16)
 
-    attended32, row_max, row_total = attention_forward(flags, queries, keys_all, values_all, score_scale)
+    attended32, row_max, row_total = attention_forward(
+        flags, queries, keys_all, values_all, grad_heads, score_scale
+    )
     attended = attended32.astype(jnp.bfloat16)
     spread = jnp.broadcast_to(attended[None], (tp_len,) + attended.shape)
     att_parts = lax.all_to_all(spread, "tp", 0, 0, tiled=True)

time: 454 us -> 415 us (0.914)
  waiting for transfers between devices: 206 us -> 148 us
  blocking collectives: 0 us -> 29.6 us
  other arithmetic: 25.5 us -> 17.2 us
  starting transfers between devices: 84.8 us -> 79 us
  local copies, waits for them, and re-layouts: 21.4 us -> 26.5 us
    all_to_all x1, waiting for transfers between devices: 48.3 us -> 0.01 us  [local(): lax.all_to_all(grad_part.astype(jnp.bfloat16).reshape(block_len, tp_len,...]
    all_to_all x1, waiting for transfers between devices: 50.4 us -> 4.55 us  [local(): att_parts = lax.all_to_all(spread, 'tp', 0, 0, tiled=True)]
    ppermute x8, waiting for transfers between devices: 89.3 us -> 126 us  [passed_along(): lax.ppermute(value, axis, [(source, source + steps) for source in range(i...]
    all_to_all x0 -> x1, blocking collectives: none -> 29.6 us  [local(): lax.all_to_all(out_weight, 'tp', split_axis=1, concat_axis=0, tiled=True)]
    convert_element_type x4, other arithmetic: 5.95 us -> 0.63 us  [local(): arrived = passed_along(back, 'ctx', -(1 << level)).astype(jnp.float32)]
    all_to_all x1 -> x0, starting transfers between devices: 5.3 us -> none  [local(): lax.all_to_all(out_weight, 'tp', split_axis=1, concat_axis=0, tiled=True)]
    unnamed x22 -> x32, local copies, waits for them, and re-layouts: 12.9 us -> 14 us
  transfers between devices with their start and end apart: 13 -> 12, of which waited for: 9 -> 7; matrix products, arithmetic and copies ran while one was open for 12% -> 7% of each run, Pallas kernels for 21% -> 11%
where the time goes in v2:
time: 415 us; the launch traced here: 414 us
  waiting for transfers between devices  148 us (36%)
  Pallas kernels  96.8 us (23%)
  starting transfers between devices  79 us (19%)
  blocking collectives  29.6 us (7%)
  local copies, waits for them, and re-layouts  26.5 us (6%)
  other arithmetic  17.2 us (4%)
  matrix products  13.2 us (3%)
    ppermute x8, waiting for transfers between devices, passed_along(): lax.ppermute(value, axis, [(source, source + steps) for source in range(i...  126 us
    pallas_call x1, Pallas kernels, attention_forward(): pl.pallas_call(kernel, grid_spec=pltpu.PrefetchScalarGridSpec(num_scalar_...  51.1 us
    pallas_call x1, Pallas kernels, attention_backward(): pl.pallas_call(kernel, grid_spec=pltpu.PrefetchScalarGridSpec(num_scalar_...  45.8 us
    ppermute x1, starting transfers between devices, local(): d_weight = lax.ppermute(reduced, ('ctx', 'tp'), moves)  37.7 us
    all_to_all x1, blocking collectives, local(): lax.all_to_all(out_weight, 'tp', split_axis=1, concat_axis=0, tiled=True)  29.6 us
    ppermute x8, starting transfers between devices, passed_along(): lax.ppermute(value, axis, [(source, source + steps) for source in range(i...  25.9 us
    ppermute x1, waiting for transfers between devices, local(): d_weight = lax.ppermute(reduced, ('ctx', 'tp'), moves)  17 us
    unnamed x32, local copies, waits for them, and re-layouts  14 us
  transfers between devices with their start and end apart: 12, of which 7 were waited for; matrix products, arithmetic and copies ran while one was open for 7% of the time, Pallas kernels for 11%

profile of v2, /device:TPU:43, one launch (start us, length us, event | category | flops | bytes accessed | tf_op | source)
XLA Modules:
  0.0 413.8 jit_solution(15909303396167138549)
XLA Ops:
  0.6 4.2 %copy.15 = bf16[256,4096]{0,1:T(8,128)(2,1)} copy(bf16[256,4096]{1,0:T(8,128)(2,1)} %param.9) | data formatting | bytes 4194304 | tf_op args[3]
  4.8 2.9 copy.16
  7.7 29.6 %all_to_all.34 = bf16[256,8,512]{2,0,1:T(8,128)(2,1)S(1)} all-to-all(bf16[256,8,512]{2,0,1:T(8,128)(2,1)S(1)} %copy.16), channel_id=1, replica_groups=mesh['ctx'=16,'tp'=8] {'tp'}, dimensions={1} | all-to-all | bytes 4194304 | tf_op jit(solution)/shard_map/all_to_all | solution.py:176
  37.3 2.4 convolution_convert_fusion
  39.7 2.3 copy.22
  42.0 5.8 %all-to-all-start.1 = ((bf16[1024,8,256]{2,0,1:T(8,128)(2,1)}), bf16[1024,8,256]{2,0,1:T(8,128)(2,1)}, u32[]{:S(2)}, u32[]{:S(2)}) async-start(bf16[1024,8,256]{2,0,1:T(8,128)(2,1)} %bitcast.34), calls=%async_computation.1 | async-start | bytes 8388608 | tf_op jit(solution)/shard_map/all_to_all | solution.py:180
  47.8 5.9 %collective-permute-start = (bf16[2,1024,256]{2,1,0:T(8,128)(2,1)S(1)}, bf16[2,1024,256]{2,1,0:T(8,128)(2,1)}, u32[]{:S(2)}, u32[]{:S(2)}) collective-permute-start(bf16[2,1024,256]{2,1,0:T(8,128)(2,1)S(1)} %pad_maximum_fusion.1), channel_id=1, source_target_pairs={{0,8},{8,16},{16,24},{24,32},{32,40},{40,48},{48,56},{56,64},{64,7... | collective-permute-start | bytes 3145736 | tf_op jit(solution)/shard_map/ppermute | solution.py:19
  53.7 4.2 %collective-permute-start.1 = (bf16[2,1024,256]{2,1,0:T(8,128)(2,1)S(1)}, bf16[2,1024,256]{2,1,0:T(8,128)(2,1)}, u32[]{:S(2)}, u32[]{:S(2)}) collective-permute-start(bf16[2,1024,256]{2,1,0:T(8,128)(2,1)S(1)} %pad_maximum_fusion.1), channel_id=1, source_target_pairs={{0,16},{8,24},{16,32},{24,40},{32,48},{40,56},{48,64},{56,72},{64,... | collective-permute-start | bytes 3145736 | tf_op jit(solution)/shard_map/ppermute | solution.py:19
  58.0 3.4 collective-permute-start.3
  68.3 45.9 %collective-permute-done = bf16[2,1024,256]{2,1,0:T(8,128)(2,1)} collective-permute-done((bf16[2,1024,256]{2,1,0:T(8,128)(2,1)S(1)}, bf16[2,1024,256]{2,1,0:T(8,128)(2,1)}, u32[]{:S(2)}, u32[]{:S(2)}) %collective-permute-start) | collective-permute-done | bytes 1048608 | tf_op jit(solution)/shard_map/ppermute | solution.py:19
  114.2 2.3 slice_dynamic-update-slice_fusion.3
  116.5 12.8 %collective-permute-done.1 = bf16[2,1024,256]{2,1,0:T(8,128)(2,1)} collective-permute-done((bf16[2,1024,256]{2,1,0:T(8,128)(2,1)S(1)}, bf16[2,1024,256]{2,1,0:T(8,128)(2,1)}, u32[]{:S(2)}, u32[]{:S(2)}) %collective-permute-start.1) | collective-permute-done | bytes 1048608 | tf_op jit(solution)/shard_map/ppermute | solution.py:19
  129.3 2.3 slice_dynamic-update-slice_fusion.2
  131.6 10.1 %collective-permute-done.2 = bf16[2,1024,256]{2,1,0:T(8,128)(2,1)} collective-permute-done((bf16[2,1024,256]{2,1,0:T(8,128)(2,1)S(1)}, bf16[2,1024,256]{2,1,0:T(8,128)(2,1)}, u32[]{:S(2)}, u32[]{:S(2)}) %collective-permute-start.2) | collective-permute-done | bytes 1048608 | tf_op jit(solution)/shard_map/ppermute | solution.py:19
  141.7 2.3 slice_dynamic-update-slice_fusion.1
  146.2 3.7 reduce_sum.71.after_ref.g_ref
  149.9 51.1 %shard_map.101 = (f32[1024,256]{1,0:T(8,128)}, f32[2,1024,128]{2,1,0:T(8,128)}, f32[2,1024,128]{2,1,0:T(8,128)}) custom-call(s32[5]{0:T(128)} %convert_element_type.36.flag_ref, bf16[1024,256]{1,0:T(8,128)(2,1)} %q_ref.3, bf16[5,1024,256]{2,1,0:T(8,128)(2,1)} %get-tuple-element.34.k_ref, bf16[5,1024,256]{2,1,0:T(8,128)(2,1)} %get-tuple-element.33.v_ref, ...), custom_call_target="tpu_custom_call" | custom-call | tf_op jit(solution)/shard_map/pallas_call | solution.py:103
  202.2 2.3 broadcast_in_dim.19
  204.5 5.1 %all-to-all-start.2 = ((bf16[8,1024,256]{2,1,0:T(8,128)(2,1)}), bf16[8,1024,256]{2,1,0:T(8,128)(2,1)}, u32[]{:S(2)}, u32[]{:S(2)}) async-start(bf16[8,1024,256]{2,1,0:T(8,128)(2,1)} %broadcast_in_dim.19), calls=%async_computation.2 | async-start | bytes 8388608 | tf_op jit(solution)/shard_map/all_to_all | solution.py:190
  209.6 45.8 %shard_map.102 = (f32[1024,256]{1,0:T(8,128)}, f32[5,1024,256]{2,1,0:T(8,128)}, f32[5,1024,256]{2,1,0:T(8,128)}) custom-call(s32[5]{0:T(128)} %convert_element_type.36.flag_ref, bf16[1024,256]{1,0:T(8,128)(2,1)} %q_ref.3, bf16[5,1024,256]{2,1,0:T(8,128)(2,1)} %get-tuple-element.34.k_ref, bf16[5,1024,256]{2,1,0:T(8,128)(2,1)} %get-tuple-element.33.v_ref, ...), custom_call_target="tpu_custom_call" | custom-call | tf_op jit(solution)/shard_map/pallas_call | solution.py:134
  255.3 2.9 convert.21
  262.3 4.5 %all-to-all-done.2 = bf16[8,1024,256]{2,1,0:T(8,128)(2,1)} async-done(((bf16[8,1024,256]{2,1,0:T(8,128)(2,1)}), bf16[8,1024,256]{2,1,0:T(8,128)(2,1)}, u32[]{:S(2)}, u32[]{:S(2)}) %all-to-all-start.2) | async-done | bytes 4194336 | tf_op jit(solution)/shard_map/all_to_all | solution.py:190
  266.9 4.6 %convolution_convert_fusion.1 = bf16[8,256,512]{2,1,0:T(8,128)(2,1)S(1)} fusion(bf16[8,1024,256]{2,1,0:T(8,128)(2,1)} %all-to-all-done.2, bf16[1024,512]{1,0:T(8,128)(2,1)S(1)} %copy-done), kind=kOutput, calls=%fused_computation.7 | convolution fusion | flops 2148532224 | bytes 7340032 | tf_op jit(solution)/shard_map/ktc,tf->kcf/dot_general | solution.py:198
  273.0 4.6 %all-to-all-start.3 = ((bf16[16,256,256]{2,1,0:T(8,128)(2,1)}), bf16[16,256,256]{2,1,0:T(8,128)(2,1)S(1)}, u32[]{:S(2)}, u32[]{:S(2)}) async-start(bf16[16,256,256]{2,1,0:T(8,128)(2,1)} %bitcast.35), calls=%async_computation.3 | async-start | bytes 4194304 | tf_op jit(solution)/shard_map/all_to_all | solution.py:206
  277.8 4.7 %collective-permute-start.5 = (bf16[2,1024,256]{2,1,0:T(8,128)(2,1)S(1)}, bf16[2,1024,256]{2,1,0:T(8,128)(2,1)S(1)}, u32[]{:S(2)}, u32[]{:S(2)}) collective-permute-start(bf16[2,1024,256]{2,1,0:T(8,128)(2,1)S(1)} %pad_maximum_fusion.3), channel_id=1, source_target_pairs={{16,0},{24,8},{32,16},{40,24},{48,32},{56,40},{64,48},{72,56},{80,... | collective-permute-start | bytes 3145736 | tf_op jit(solution)/shard_map/ppermute | solution.py:19
  287.3 2.6 collective-permute-start.4
  289.9 36.6 %collective-permute-done.5 = bf16[2,1024,256]{2,1,0:T(8,128)(2,1)S(1)} collective-permute-done((bf16[2,1024,256]{2,1,0:T(8,128)(2,1)S(1)}, bf16[2,1024,256]{2,1,0:T(8,128)(2,1)S(1)}, u32[]{:S(2)}, u32[]{:S(2)}) %collective-permute-start.5) | collective-permute-done | bytes 1048608 | tf_op jit(solution)/shard_map/ppermute | solution.py:19
  326.9 21.0 %collective-permute-done.7 = bf16[2,1024,256]{2,1,0:T(8,128)(2,1)S(1)} collective-permute-done((bf16[2,1024,256]{2,1,0:T(8,128)(2,1)S(1)}, bf16[2,1024,256]{2,1,0:T(8,128)(2,1)S(1)}, u32[]{:S(2)}, u32[]{:S(2)}) %collective-permute-start.7) | collective-permute-done | bytes 1048608 | tf_op jit(solution)/shard_map/ppermute | solution.py:19
  348.2 3.7 fusion.4
  352.2 37.7 %collective-permute-start.8 = (f32[256,256]{1,0:T(8,128)S(1)}, f32[256,256]{1,0:T(8,128)S(1)}, u32[]{:S(2)}, u32[]{:S(2)}) collective-permute-start(f32[256,256]{1,0:T(8,128)S(1)} %convert_reduce_fusion), channel_id=1, source_target_pairs={{0,0},{1,16},{2,32},{3,48},{4,64},{5,80},{6,96},{7,112},{8,8},{9,2... | collective-permute-start | bytes 786440 | tf_op jit(solution)/shard_map/ppermute | solution.py:211
  389.8 6.2 %bitcast_convert_fusion = bf16[1024,512]{1,0:T(8,128)(2,1)} fusion(bf16[8,1024,256]{2,1,0:T(8,128)(2,1)} %all-to-all-done.2, bf16[256,8,512]{2,0,1:T(8,128)(2,1)} %copy-done.3), kind=kOutput, calls=%fused_computation.4 | convolution fusion | flops 2148007936 | bytes 7340032 | tf_op jit(solution)/shard_map/ktc,kcf->tf/dot_general | solution.py:191
  396.1 17.0 %collective-permute-done.8 = f32[256,256]{1,0:T(8,128)S(1)} collective-permute-done((f32[256,256]{1,0:T(8,128)S(1)}, f32[256,256]{1,0:T(8,128)S(1)}, u32[]{:S(2)}, u32[]{:S(2)}) %collective-permute-start.8) | collective-permute-done | bytes 262176 | tf_op jit(solution)/shard_map/ppermute | solution.py:211
  (58 shorter events, 20.1 us)
Async XLA Ops:
  0.6 36.7 %copy-start = (bf16[1024,512]{1,0:T(8,128)(2,1)S(1)}, bf16[1024,512]{1,0:T(8,128)(2,1)}, u32[]{:S(2)}) copy-start(bf16[1024,512]{1,0:T(8,128)(2,1)} %param.10) | copy-start | bytes 3145732
  37.3 2.4 copy-start.3
  42.0 5.8 %copy-start.4 = (bf16[1024,256]{1,0:T(8,128)(2,1)S(1)}, bf16[1024,256]{1,0:T(8,128)(2,1)}, u32[]{:S(2)}) copy-start(bf16[1024,256]{1,0:T(8,128)(2,1)} %param.7) | copy-start | bytes 1572868
  42.0 5.8 %copy-start.5 = (bf16[1024,256]{1,0:T(8,128)(2,1)S(1)}, bf16[1024,256]{1,0:T(8,128)(2,1)}, u32[]{:S(2)}) copy-start(bf16[1024,256]{1,0:T(8,128)(2,1)} %param.8) | copy-start | bytes 1572868
  42.0 21.3 %copy-start.12 = (s32[16,16]{1,0:T(8,128)S(1)}, s32[16,16]{1,0:T(8,128)}, u32[]{:S(2)}) copy-start(s32[16,16]{1,0:T(8,128)} %param.11) | copy-start | bytes 3076
  42.0 104.2 %all-to-all-start.1 = ((bf16[1024,8,256]{2,0,1:T(8,128)(2,1)}), bf16[1024,8,256]{2,0,1:T(8,128)(2,1)}, u32[]{:S(2)}, u32[]{:S(2)}) async-start(bf16[1024,8,256]{2,0,1:T(8,128)(2,1)} %bitcast.34), calls=%async_computation.1 | async-start | bytes 8388608 | tf_op jit(solution)/shard_map/all_to_all | solution.py:180
  47.8 66.4 %collective-permute-start = (bf16[2,1024,256]{2,1,0:T(8,128)(2,1)S(1)}, bf16[2,1024,256]{2,1,0:T(8,128)(2,1)}, u32[]{:S(2)}, u32[]{:S(2)}) collective-permute-start(bf16[2,1024,256]{2,1,0:T(8,128)(2,1)S(1)} %pad_maximum_fusion.1), channel_id=1, source_target_pairs={{0,8},{8,16},{16,24},{24,32},{32,40},{40,48},{48,56},{56,64},{64,7... | collective-permute-start | bytes 3145736 | tf_op jit(solution)/shard_map/ppermute | solution.py:19
  53.7 75.5 %collective-permute-start.1 = (bf16[2,1024,256]{2,1,0:T(8,128)(2,1)S(1)}, bf16[2,1024,256]{2,1,0:T(8,128)(2,1)}, u32[]{:S(2)}, u32[]{:S(2)}) collective-permute-start(bf16[2,1024,256]{2,1,0:T(8,128)(2,1)S(1)} %pad_maximum_fusion.1), channel_id=1, source_target_pairs={{0,16},{8,24},{16,32},{24,40},{32,48},{40,56},{48,64},{56,72},{64,... | collective-permute-start | bytes 3145736 | tf_op jit(solution)/shard_map/ppermute | solution.py:19
  58.0 86.0 %collective-permute-start.3 = (bf16[2,1024,256]{2,1,0:T(8,128)(2,1)S(1)}, bf16[2,1024,256]{2,1,0:T(8,128)(2,1)}, u32[]{:S(2)}, u32[]{:S(2)}) collective-permute-start(bf16[2,1024,256]{2,1,0:T(8,128)(2,1)S(1)} %pad_maximum_fusion.1), channel_id=1, source_target_pairs={{0,64},{8,72},{16,80},{24,88},{32,96},{40,104},{48,112},{56,120},{... | collective-permute-start | bytes 3145736 | tf_op jit(solution)/shard_map/ppermute | solution.py:19
  61.3 80.3 %collective-permute-start.2 = (bf16[2,1024,256]{2,1,0:T(8,128)(2,1)S(1)}, bf16[2,1024,256]{2,1,0:T(8,128)(2,1)}, u32[]{:S(2)}, u32[]{:S(2)}) collective-permute-start(bf16[2,1024,256]{2,1,0:T(8,128)(2,1)S(1)} %pad_maximum_fusion.1), channel_id=1, source_target_pairs={{0,32},{8,40},{16,48},{24,56},{32,64},{40,72},{48,80},{56,88},{64,... | collective-permute-start | bytes 3145736 | tf_op jit(solution)/shard_map/ppermute | solution.py:19
  204.5 62.4 %all-to-all-start.2 = ((bf16[8,1024,256]{2,1,0:T(8,128)(2,1)}), bf16[8,1024,256]{2,1,0:T(8,128)(2,1)}, u32[]{:S(2)}, u32[]{:S(2)}) async-start(bf16[8,1024,256]{2,1,0:T(8,128)(2,1)} %broadcast_in_dim.19), calls=%async_computation.2 | async-start | bytes 8388608 | tf_op jit(solution)/shard_map/all_to_all | solution.py:190
  255.3 4.0 copy-start.2
  273.0 4.6 %copy-start.10 = (bf16[1,1024,256]{2,1,0:T(8,128)(2,1)S(1)}, bf16[1,1024,256]{2,1,0:T(8,128)(2,1)}, u32[]{:S(2)}) copy-start(bf16[1,1024,256]{2,1,0:T(8,128)(2,1)} %get-tuple-element.26) | copy-start | bytes 1572868
  273.0 4.6 %copy-start.11 = (bf16[1,1024,256]{2,1,0:T(8,128)(2,1)S(1)}, bf16[1,1024,256]{2,1,0:T(8,128)(2,1)}, u32[]{:S(2)}) copy-start(bf16[1,1024,256]{2,1,0:T(8,128)(2,1)} %get-tuple-element.30) | copy-start | bytes 1572868
  273.0 78.8 %all-to-all-start.3 = ((bf16[16,256,256]{2,1,0:T(8,128)(2,1)}), bf16[16,256,256]{2,1,0:T(8,128)(2,1)S(1)}, u32[]{:S(2)}, u32[]{:S(2)}) async-start(bf16[16,256,256]{2,1,0:T(8,128)(2,1)} %bitcast.35), calls=%async_computation.3 | async-start | bytes 4194304 | tf_op jit(solution)/shard_map/all_to_all | solution.py:206
  277.7 8.1 %copy-start.8 = (bf16[1,1024,256]{2,1,0:T(8,128)(2,1)S(1)}, bf16[1,1024,256]{2,1,0:T(8,128)(2,1)}, u32[]{:S(2)}) copy-start(bf16[1,1024,256]{2,1,0:T(8,128)(2,1)} %get-tuple-element.24) | copy-start | bytes 1572868
  277.7 8.1 %copy-start.9 = (bf16[1,1024,256]{2,1,0:T(8,128)(2,1)S(1)}, bf16[1,1024,256]{2,1,0:T(8,128)(2,1)}, u32[]{:S(2)}) copy-start(bf16[1,1024,256]{2,1,0:T(8,128)(2,1)} %get-tuple-element.28) | copy-start | bytes 1572868
  277.8 9.4 %copy-start.6 = (bf16[1,1024,256]{2,1,0:T(8,128)(2,1)S(1)}, bf16[1,1024,256]{2,1,0:T(8,128)(2,1)}, u32[]{:S(2)}) copy-start(bf16[1,1024,256]{2,1,0:T(8,128)(2,1)} %get-tuple-element.23) | copy-start | bytes 1572868
  277.8 9.4 %copy-start.7 = (bf16[1,1024,256]{2,1,0:T(8,128)(2,1)S(1)}, bf16[1,1024,256]{2,1,0:T(8,128)(2,1)}, u32[]{:S(2)}) copy-start(bf16[1,1024,256]{2,1,0:T(8,128)(2,1)} %get-tuple-element.27) | copy-start | bytes 1572868
  277.8 48.7 %collective-permute-start.5 = (bf16[2,1024,256]{2,1,0:T(8,128)(2,1)S(1)}, bf16[2,1024,256]{2,1,0:T(8,128)(2,1)S(1)}, u32[]{:S(2)}, u32[]{:S(2)}) collective-permute-start(bf16[2,1024,256]{2,1,0:T(8,128)(2,1)S(1)} %pad_maximum_fusion.3), channel_id=1, source_target_pairs={{16,0},{24,8},{32,16},{40,24},{48,32},{56,40},{64,48},{72,56},{80,... | collective-permute-start | bytes 3145736 | tf_op jit(solution)/shard_map/ppermute | solution.py:19
  283.9 42.8 %collective-permute-start.6 = (bf16[2,1024,256]{2,1,0:T(8,128)(2,1)S(1)}, bf16[2,1024,256]{2,1,0:T(8,128)(2,1)S(1)}, u32[]{:S(2)}, u32[]{:S(2)}) collective-permute-start(bf16[2,1024,256]{2,1,0:T(8,128)(2,1)S(1)} %pad_maximum_fusion.4), channel_id=1, source_target_pairs={{32,0},{40,8},{48,16},{56,24},{64,32},{72,40},{80,48},{88,56},{96,... | collective-permute-start | bytes 3145736 | tf_op jit(solution)/shard_map/ppermute | solution.py:19
  285.9 61.9 %collective-permute-start.7 = (bf16[2,1024,256]{2,1,0:T(8,128)(2,1)S(1)}, bf16[2,1024,256]{2,1,0:T(8,128)(2,1)S(1)}, u32[]{:S(2)}, u32[]{:S(2)}) collective-permute-start(bf16[2,1024,256]{2,1,0:T(8,128)(2,1)S(1)} %pad_maximum_fusion.5), channel_id=1, source_target_pairs={{64,0},{72,8},{80,16},{88,24},{96,32},{104,40},{112,48},{120,56},{... | collective-permute-start | bytes 3145736 | tf_op jit(solution)/shard_map/ppermute | solution.py:19
  287.3 60.6 %collective-permute-start.4 = (bf16[2,1024,256]{2,1,0:T(8,128)(2,1)S(1)}, bf16[2,1024,256]{2,1,0:T(8,128)(2,1)S(1)}, u32[]{:S(2)}, u32[]{:S(2)}) collective-permute-start(bf16[2,1024,256]{2,1,0:T(8,128)(2,1)S(1)} %pad_maximum_fusion.2), channel_id=1, source_target_pairs={{8,0},{16,8},{24,16},{32,24},{40,32},{48,40},{56,48},{64,56},{72,6... | collective-permute-start | bytes 3145736 | tf_op jit(solution)/shard_map/ppermute | solution.py:19
  352.2 60.9 %collective-permute-start.8 = (f32[256,256]{1,0:T(8,128)S(1)}, f32[256,256]{1,0:T(8,128)S(1)}, u32[]{:S(2)}, u32[]{:S(2)}) collective-permute-start(f32[256,256]{1,0:T(8,128)S(1)} %convert_reduce_fusion), channel_id=1, source_target_pairs={{0,0},{1,16},{2,32},{3,48},{4,64},{5,80},{6,96},{7,112},{8,8},{9,2... | collective-permute-start | bytes 786440 | tf_op jit(solution)/shard_map/ppermute | solution.py:211
  389.8 24.0 %copy-start.1 = (bf16[1024,512]{1,0:T(8,128)(2,1)S(1)}, bf16[1024,512]{1,0:T(8,128)(2,1)}, u32[]{:S(2)}) copy-start(bf16[1024,512]{1,0:T(8,128)(2,1)} %param.10) | copy-start | bytes 3145732
